TPU v7x, 32 devices: a whole 2x2x4 slice. The times are simulated.
32 devices in a mesh: leaf: 8 (over z, x), panel: 4 (over y, core).
Axes of the slice: x: 2, y: 2, z: 4, core: 2. Of those that a mesh axis runs over, the one named last changes fastest.
Arguments:
- upper_rhs: float32 [8, 512, 128], P('leaf'), may hold values from -6 to 6
- upper_panel: float32 [8, 1024, 512], P('leaf', 'panel'), may hold values from -0.25 to 0.25
- upper_inverse: float32 [8, 512, 512], P('leaf'), as said below
- top_index: int32 [8, 1024], P('leaf', 'panel'), may hold values from 0 to 511
- top_solution: float32 [512, 128], P(('leaf', 'panel')), may hold values from -6 to 6
- owner_map: int32 [8], replicated, may hold values from 0 to 7, each once
- parent_list: int32 [256], P(('leaf', 'panel')), may hold values from 0 to 7, as said below
- lower_index: int32 [256, 256], P(('leaf', 'panel')), may hold values from 0 to 511
- lower_panel: float32 [256, 256, 256], P(('leaf', 'panel')), may hold values from -0.5 to 0.5
- lower_rhs: float32 [256, 256, 128], P(('leaf', 'panel')), may hold values from -6 to 6
- lower_inverse: float32 [256, 256, 256], P(('leaf', 'panel')), as said below
Outputs:
- upper_solution: float32 [8, 512, 128], P('leaf', 'panel')
- lower_solution: float32 [256, 256, 128], P(('leaf', 'panel'))
Inputs may be any that keep to these rules, and one draw needn't show every extreme that they name: `owner_map`: each leaf index holds exactly one upper supernode. `parent_list`: the 8 lower supernodes of one device have pairwise different parents. `upper_inverse`: lower triangular with a positive diagonal. `lower_inverse`: lower triangular with a positive diagonal.
All inputs are finite; a program needn't handle non-finite values.
Results may differ from a plain program's by a relative error of at most 0.00007.
Values sent between devices are 32-bit elements; how exact they have to be, the bound alone decides.
No kernel may reach another device: no remote copies, remote signals or barrier semaphores. Data moves between devices by JAX's collectives and lax.ppermute only.
A program may use at most 64 MiB of HBM per device.

v0:
```python
import jax
import jax.numpy as jnp
from jax import lax
from jax.sharding import PartitionSpec as P


def local(
    upper_rhs,
    upper_panel,
    upper_inverse,
    top_index,
    top_solution,
    owner_map,
    parent_list,
    lower_index,
    lower_panel,
    lower_rhs,
    lower_inverse,
):
    highest = lax.Precision.HIGHEST
    panels = lax.axis_size("panel")
    panel_index = lax.axis_index("panel")
    width_upper = upper_rhs.shape[1]
    share = width_upper // panels
    begin = panel_index * share
    top_whole = lax.all_gather(top_solution, ("leaf", "panel"), axis=0, tiled=True)
    gathered = top_whole[top_index[0]]
    panel_rows = upper_panel[0]
    partial_update = jnp.einsum("kw,kr->wr", panel_rows, gathered, precision=highest)
    update = lax.psum(partial_update, "panel")
    reduced = upper_rhs[0] - update
    full_solution = jnp.einsum("kw,kr->wr", upper_inverse[0], reduced, precision=highest)
    own_rows = lax.dynamic_slice_in_dim(full_solution, begin, share, 0)
    position = owner_map[parent_list]
    all_upper = lax.all_gather(full_solution[None], "leaf", axis=0, tiled=True)
    parent_rows = all_upper[position[:, None], lower_index]
    lower_update = jnp.einsum("skw,skr->swr", lower_panel, parent_rows, precision=highest)
    lower_solution = jnp.einsum(
        "skw,skr->swr", lower_inverse, lower_rhs - lower_update, precision=highest
    )
    return (own_rows[None], lower_solution)


def solution(mesh):
    placed = (
        P("leaf", None, None),
        P("leaf", "panel", None),
        P("leaf", None, None),
        P("leaf", "panel"),
        P(("leaf", "panel"), None),
        P(),
        P(("leaf", "panel")),
        P(("leaf", "panel"), None),
        P(("leaf", "panel"), None, None),
        P(("leaf", "panel"), None, None),
        P(("leaf", "panel"), None, None),
    )
    return jax.shard_map(
        local,
        mesh=mesh,
        in_specs=placed,
        out_specs=(P("leaf", "panel", None), P(("leaf", "panel"), None, None)),
        check_vma=False,
    )
```

profile of v0, /device:TPU:0, one launch (start us, length us, event | category | flops | bytes accessed | tf_op | source)
XLA Modules:
  0.0 174.9 jit_solution(9198700522070792228)
XLA Ops:
  7.2 0.0 copy-start
  7.2 0.0 copy-start.3
  7.2 0.0 all-reduce.2.cloned.1.call-start
  7.2 44.3 %all_gather.6 = f32[512,128]{1,0:T(8,128)S(1)} all-gather(f32[16,128]{1,0:T(8,128)} %param.15), channel_id=1, replica_groups=mesh['leaf'=8,'panel'=4] {'leaf','panel'}, dimensions={0}, use_global_device_ids=true | all-gather | bytes 270336 | tf_op jit(solution)/shard_map/all_gather | solution.py:26
  51.5 0.7 compare_select_fusion.1
  52.2 0.0 copy-start.5
  52.2 0.0 copy-start.1
  52.3 0.7 gather_fusion
  53.0 0.0 copy-start.4
  53.0 2.8 %convolution_bitcast_fusion.2 = f32[512,128]{1,0:T(8,128)} fusion(f32[256,128]{1,0:T(8,128)S(1)} %gather_fusion, f32[1,256,512]{2,1,0:T(8,128)} %param.12), kind=kOutput, calls=%fused_computation.6 | convolution fusion | flops 201326592 | bytes 917504 | tf_op jit(solution)/shard_map/kw,kr->wr/dot_general | solution.py:29
  55.8 0.0 all-reduce.2.cloned.1.call-update
  55.8 0.0 all-gather.3.cloned.1.call-start
  55.8 28.2 %all-reduce.2.cloned.1.call-done = f32[512,128]{1,0:T(8,128)} async-done(((f32[512,128]{1,0:T(8,128)}), f32[512,128]{1,0:T(8,128)}) %all-reduce.2.cloned.1.call-update) | async-done | bytes 262160 | tf_op jit(solution)/shard_map/psum | solution.py:30
  84.0 0.0 copy-done.3
  84.0 2.5 %fusion.1 = f32[128,512]{1,0:T(8,128)} fusion(f32[1,512,512]{2,1,0:T(8,128)S(1)} %copy-done.3, f32[512,128]{1,0:T(8,128)} %all-reduce.2.cloned.1.call-done, f32[1,512,128]{2,1,0:T(8,128)} %param.11), kind=kOutput, calls=%fused_computation.7 | convolution fusion | flops 402718720 | bytes 1835008 | tf_op jit(solution)/shard_map/kw,kr->wr/dot_general | solution.py:32
  86.5 0.0 all-gather.3.cloned.1.call-update
  86.6 0.0 copy-done.5
  86.6 0.0 copy-done.1
  86.6 0.6 gather_fusion.1
  87.3 0.0 copy-done.4
  87.3 0.1 fusion.8
  87.3 0.8 dynamic-slice_bitcast_fusion
  88.2 0.7 copy.19
  88.9 47.4 %all-gather.3.cloned.1.call-done = f32[4096,128]{0,1:T(8,128)} async-done(((f32[512,128]{0,1:T(8,128)}), f32[4096,128]{0,1:T(8,128)}) %all-gather.3.cloned.1.call-update) | async-done | bytes 2097168 | tf_op jit(solution)/shard_map/all_gather | solution.py:35
  136.3 2.9 %copy.22 = f32[4096,128]{1,0:T(8,128)} copy(f32[4096,128]{0,1:T(8,128)} %all-gather.3.cloned.1.call-done) | data formatting | bytes 4194304 | tf_op jit(solution)/shard_map/all_gather | solution.py:35
  139.2 20.6 %gather_fusion.2 = f32[2048,128]{1,0:T(8,128)S(1)} fusion(f32[8,512,128]{2,1,0:T(8,128)} %bitcast.43, s32[2048]{0:T(1024)S(1)} %bitcast.42), kind=kCustom, calls=%fused_computation.2 | custom fusion | bytes 2113536 | tf_op jit(solution)/shard_map/gather | solution.py:36
  159.8 0.0 copy-done
  159.8 0.0 copy-start.2
  159.8 4.9 %fusion = f32[8,256,128]{2,1,0:T(8,128)S(1)} fusion(f32[8,256,128]{2,1,0:T(8,128)} %param.20, f32[8,256,128]{2,1,0:T(8,128)S(1)} %bitcast.44, f32[8,256,256]{2,1,0:T(8,128)S(1)} %copy-done), kind=kOutput, calls=%fused_computation.5 | convolution fusion | flops 805568512 | bytes 5242880 | tf_op jit(solution)/shard_map/skw,skr->swr/dot_general | solution.py:37
  164.7 0.0 copy-done.2
  164.7 2.0 %convolution_bitcast_fusion = f32[8,256,128]{1,2,0:T(8,128)S(1)} fusion(f32[8,256,128]{2,1,0:T(8,128)S(1)} %fusion, f32[8,256,256]{2,1,0:T(8,128)S(1)} %copy-done.2), kind=kOutput, calls=%fused_computation.3 | convolution fusion | flops 805306368 | bytes 4194304 | tf_op jit(solution)/shard_map/skw,skr->swr/dot_general | solution.py:38
  166.7 1.3 copy.20
  (5 shorter events, 0.0 us)
Async XLA Ops:
  7.2 152.6 %copy-start = (f32[8,256,256]{2,1,0:T(8,128)S(1)}, f32[8,256,256]{2,1,0:T(8,128)}, u32[]{:S(2)}) copy-start(f32[8,256,256]{2,1,0:T(8,128)} %param.19) | copy-start | bytes 6291460
  7.2 76.8 %copy-start.3 = (f32[1,512,512]{2,1,0:T(8,128)S(1)}, f32[1,512,512]{2,1,0:T(8,128)}, u32[]{:S(2)}) copy-start(f32[1,512,512]{2,1,0:T(8,128)} %param.13) | copy-start | bytes 3145732
  7.2 76.8 %all-reduce.2.cloned.1.call-start = ((), (), s32[]{:S(2)}) async-start(), calls=%async_computation | async-start | bytes 524288 | tf_op jit(solution)/shard_map/psum | solution.py:30
  52.2 34.3 %copy-start.5 = (s32[8]{0:T(128)S(1)}, s32[8]{0:T(128)}, u32[]{:S(2)}) copy-start(s32[8]{0:T(128)} %param.17) | copy-start | bytes 100
  52.2 34.3 %copy-start.1 = (s32[8]{0:T(128)S(1)}, s32[8]{0:T(128)}, u32[]{:S(2)}) copy-start(s32[8]{0:T(128)} %param.16) | copy-start | bytes 100
  53.0 34.3 %copy-start.4 = (s32[8,256]{1,0:T(8,128)S(1)}, s32[8,256]{1,0:T(8,128)}, u32[]{:S(2)}) copy-start(s32[8,256]{1,0:T(8,128)} %param.18) | copy-start | bytes 24580
  55.8 80.5 %all-gather.3.cloned.1.call-start = ((), (), s32[]{:S(2)}) async-start(), calls=%async_computation.1 | async-start | bytes 2359296 | tf_op jit(solution)/shard_map/all_gather | solution.py:35
  159.8 4.9 %copy-start.2 = (f32[8,256,256]{2,1,0:T(8,128)S(1)}, f32[8,256,256]{2,1,0:T(8,128)}, u32[]{:S(2)}) copy-start(f32[8,256,256]{2,1,0:T(8,128)} %param.21) | copy-start | bytes 6291460
Sparse Core Ops, SparseCore 0:
  55.9 28.0 all-reduce.1
  87.0 49.2 all-gather.2
where the time goes:
time: 175 us
  waiting for transfers between devices  75.6 us (43%)
  blocking collectives  44.3 us (25%)
  local copies, waits for them, and re-layouts  27.8 us (16%)
  between operations  14.2 us (8%)
  matrix products  12.2 us (7%)
    all_gather x1, waiting for transfers between devices, local(): all_upper = lax.all_gather(full_solution[None], 'leaf', axis=0, tiled=True)  47.4 us
    all_gather x1, blocking collectives, local(): lax.all_gather(top_solution, ('leaf', 'panel'), axis=0, tiled=True)  44.3 us
    psum x1, waiting for transfers between devices, local(): update = lax.psum(partial_update, 'panel')  28.2 us
    gather x1, local copies, waits for them, and re-layouts, local(): parent_rows = all_upper[position[:, None], lower_index]  20.6 us
    dot_general x1, matrix products, local(): jnp.einsum('skw,skr->swr', lower_panel, parent_rows, precision=highest)  4.89 us
  transfers between devices with their start and end apart: 2, of which 2 were waited for; matrix products, arithmetic and copies ran while one was open for 1% of the time, Pallas kernels for 0%

commit v1 on v0

--- a/solution.py
+++ b/solution.py
@@ -32,7 +32,18 @@
     full_solution = jnp.einsum("kw,kr->wr", upper_inverse[0], reduced, precision=highest)
     own_rows = lax.dynamic_slice_in_dim(full_solution, begin, share, 0)
     position = owner_map[parent_list]
-    all_upper = lax.all_gather(full_solution[None], "leaf", axis=0, tiled=True)
+    ways = lax.axis_size("leaf")
+    up = [(d, (d + 1) % ways) for d in range(ways)]
+    down = [(d, (d - 1) % ways) for d in range(ways)]
+    earlier, later = ([full_solution[None]], [full_solution[None]])
+    for _ in range(ways // 2):
+        earlier.append(lax.ppermute(earlier[-1], "leaf", up))
+    for _ in range((ways - 1) // 2):
+        later.append(lax.ppermute(later[-1], "leaf", down))
+    line = jnp.concatenate([*earlier[::-1], *later[1:]], axis=0)
+    all_upper = jnp.roll(
+        line, (lax.axis_index("leaf") - ways // 2) * full_solution[None].shape[0], axis=0
+    )
     parent_rows = all_upper[position[:, None], lower_index]
     lower_update = jnp.einsum("skw,skr->swr", lower_panel, parent_rows, precision=highest)
     lower_solution = jnp.einsum(

time: 175 us -> 177 us (1.011); the launches traced: 175 us -> 175 us
  waiting for transfers between devices: 75.6 us -> 54.7 us
  starting transfers between devices: 0.08 us -> 16.7 us
  local copies, waits for them, and re-layouts: 27.8 us -> 32.5 us
    all_gather x1 -> x0, waiting for transfers between devices: 47.4 us -> none  [local(): all_upper = lax.all_gather(full_solution[None], 'leaf', axis=0, tiled=True)]
    ppermute x0 -> x7, waiting for transfers between devices: none -> 26.4 us  [the longest x4 25 us: local(): earlier.append(lax.ppermute(earlier[-1], 'leaf', up))]
    ppermute x0 -> x7, starting transfers between devices: none -> 16.7 us  [the longest x3 10.2 us: local(): later.append(lax.ppermute(later[-1], 'leaf', down))]
    dynamic_slice x0 -> x2, local copies, waits for them, and re-layouts: none -> 4.48 us  [local(): jnp.roll(line, (lax.axis_index('leaf') - ways // 2) * full_solution[None]...]
    unnamed x15 -> x28, local copies, waits for them, and re-layouts: 2.08 us -> 6.17 us
    all_gather x1 -> x0, local copies, waits for them, and re-layouts: 2.9 us -> none  [local(): all_upper = lax.all_gather(full_solution[None], 'leaf', axis=0, tiled=True)]
  transfers between devices with their start and end apart: 2 -> 8, of which waited for: 2 -> 7; matrix products, arithmetic and copies ran while one was open for 1% -> 2% of each run, Pallas kernels for 0% -> 0%
where the time goes in v1:
time: 177 us; the launch traced here: 175 us
  waiting for transfers between devices  54.7 us (31%)
  blocking collectives  44.3 us (25%)
  local copies, waits for them, and re-layouts  32.5 us (18%)
  starting transfers between devices  16.7 us (9%)
  between operations  14.2 us (8%)
  matrix products  11.8 us (7%)
    all_gather x1, blocking collectives, local(): lax.all_gather(top_solution, ('leaf', 'panel'), axis=0, tiled=True)  44.3 us
    psum x1, waiting for transfers between devices, local(): update = lax.psum(partial_update, 'panel')  28.2 us
    ppermute x4, waiting for transfers between devices, local(): earlier.append(lax.ppermute(earlier[-1], 'leaf', up))  25 us
    gather x1, local copies, waits for them, and re-layouts, local(): parent_rows = all_upper[position[:, None], lower_index]  20.4 us
    ppermute x3, starting transfers between devices, local(): later.append(lax.ppermute(later[-1], 'leaf', down))  10.2 us
    ppermute x4, starting transfers between devices, local(): earlier.append(lax.ppermute(earlier[-1], 'leaf', up))  6.49 us
    unnamed x28, local copies, waits for them, and re-layouts  6.17 us
    dot_general x1, matrix products, local(): jnp.einsum('skw,skr->swr', lower_panel, parent_rows, precision=highest)  4.87 us
  transfers between devices with their start and end apart: 8, of which 7 were waited for; matrix products, arithmetic and copies ran while one was open for 2% of the time, Pallas kernels for 0%

profile of v1, /device:TPU:0, one launch (start us, length us, event | category | flops | bytes accessed | tf_op | source)
XLA Modules:
  0.0 175.0 jit_solution(5996773412531298202)
XLA Ops:
  7.2 0.0 copy-start
  7.2 0.0 copy-start.4
  7.2 0.0 copy-start.1
  7.2 0.0 copy-start.3
  7.2 0.0 all-reduce.2.cloned.1.call-start
  7.3 44.3 %all_gather.3 = f32[512,128]{1,0:T(8,128)S(1)} all-gather(f32[16,128]{1,0:T(8,128)} %param.15), channel_id=1, replica_groups=mesh['leaf'=8,'panel'=4] {'leaf','panel'}, dimensions={0}, use_global_device_ids=true | all-gather | bytes 270336 | tf_op jit(solution)/shard_map/all_gather | solution.py:26
  51.6 0.7 compare_select_fusion.1
  52.3 0.7 gather_fusion
  53.0 2.7 %convolution_bitcast_fusion.2 = f32[512,128]{1,0:T(8,128)} fusion(f32[256,128]{1,0:T(8,128)S(1)} %gather_fusion, f32[1,256,512]{2,1,0:T(8,128)} %param.12), kind=kOutput, calls=%fused_computation.6 | convolution fusion | flops 201326592 | bytes 917504 | tf_op jit(solution)/shard_map/kw,kr->wr/dot_general | solution.py:29
  55.7 0.0 all-reduce.2.cloned.1.call-update
  55.8 28.2 %all-reduce.2.cloned.1.call-done = f32[512,128]{1,0:T(8,128)} async-done(((f32[512,128]{1,0:T(8,128)}), f32[512,128]{1,0:T(8,128)}) %all-reduce.2.cloned.1.call-update) | async-done | bytes 262160 | tf_op jit(solution)/shard_map/psum | solution.py:30
  84.0 2.2 %fusion.1 = f32[128,512]{1,0:T(8,128)S(1)} fusion(f32[1,512,512]{2,1,0:T(8,128)} %param.13, f32[512,128]{1,0:T(8,128)} %all-reduce.2.cloned.1.call-done, f32[1,512,128]{2,1,0:T(8,128)} %param.11), kind=kOutput, calls=%fused_computation.7 | convolution fusion | flops 402718720 | bytes 1835008 | tf_op jit(solution)/shard_map/kw,kr->wr/dot_general | solution.py:32
  86.1 1.5 collective-permute-start
  87.7 7.9 %collective-permute-done = f32[1,512,128]{1,2,0:T(8,128)S(1)} collective-permute-done((f32[1,512,128]{1,2,0:T(8,128)S(1)}, f32[1,512,128]{1,2,0:T(8,128)S(1)}, u32[]{:S(2)}, u32[]{:S(2)}) %collective-permute-start) | collective-permute-done | bytes 262176 | tf_op jit(solution)/shard_map/ppermute | solution.py:40
  95.6 0.0 collective-permute-start.1
  95.6 0.0 copy-done.4
  95.6 4.7 %collective-permute-start.4 = (f32[1,512,128]{1,2,0:T(8,128)S(1)}, f32[1,512,128]{1,2,0:T(8,128)S(1)}, u32[]{:S(2)}, u32[]{:S(2)}) collective-permute-start(f32[1,512,128]{1,2,0:T(8,128)S(1)} %bitcast.48), channel_id=1, source_target_pairs={{0,28},{4,0},{8,4},{12,8},{16,12},{20,16},{24,20},{28,24},{1,29},{... | collective-permute-start | bytes 786440 | tf_op jit(solution)/shard_map/ppermute | solution.py:42
  100.3 4.5 %collective-permute-done.1 = f32[1,512,128]{1,2,0:T(8,128)S(1)} collective-permute-done((f32[1,512,128]{1,2,0:T(8,128)S(1)}, f32[1,512,128]{1,2,0:T(8,128)S(1)}, u32[]{:S(2)}, u32[]{:S(2)}) %collective-permute-start.1) | collective-permute-done | bytes 262176 | tf_op jit(solution)/shard_map/ppermute | solution.py:40
  104.8 2.5 %collective-permute-start.2 = (f32[1,512,128]{1,2,0:T(8,128)S(1)}, f32[1,512,128]{1,2,0:T(8,128)S(1)}, u32[]{:S(2)}, u32[]{:S(2)}) collective-permute-start(f32[1,512,128]{1,2,0:T(8,128)S(1)} %collective-permute-done.1), channel_id=1, source_target_pairs={{0,4},{4,8},{8,12},{12,16},{16,20},{20,24},{24,28},{28,0},{1,5},{5... | collective-permute-start | bytes 786440 | tf_op jit(solution)/shard_map/ppermute | solution.py:40
  107.3 0.0 copy-done.1
  107.3 0.6 gather_fusion.1
  108.0 0.0 collective-permute-done.4
  108.0 3.7 %collective-permute-start.5 = (f32[1,512,128]{1,2,0:T(8,128)S(1)}, f32[1,512,128]{1,2,0:T(8,128)}, u32[]{:S(2)}, u32[]{:S(2)}) collective-permute-start(f32[1,512,128]{1,2,0:T(8,128)S(1)} %collective-permute-done.4), channel_id=1, source_target_pairs={{0,28},{4,0},{8,4},{12,8},{16,12},{20,16},{24,20},{28,24},{1,29},{... | collective-permute-start | bytes 786440 | tf_op jit(solution)/shard_map/ppermute | solution.py:42
  111.6 6.5 %collective-permute-done.2 = f32[1,512,128]{1,2,0:T(8,128)S(1)} collective-permute-done((f32[1,512,128]{1,2,0:T(8,128)S(1)}, f32[1,512,128]{1,2,0:T(8,128)S(1)}, u32[]{:S(2)}, u32[]{:S(2)}) %collective-permute-start.2) | collective-permute-done | bytes 262176 | tf_op jit(solution)/shard_map/ppermute | solution.py:40
  118.2 2.5 %collective-permute-start.3 = (f32[1,512,128]{1,2,0:T(8,128)S(1)}, f32[1,512,128]{1,2,0:T(8,128)}, u32[]{:S(2)}, u32[]{:S(2)}) collective-permute-start(f32[1,512,128]{1,2,0:T(8,128)S(1)} %collective-permute-done.2), channel_id=1, source_target_pairs={{0,4},{4,8},{8,12},{12,16},{16,20},{20,24},{24,28},{28,0},{1,5},{5... | collective-permute-start | bytes 786440 | tf_op jit(solution)/shard_map/ppermute | solution.py:40
  120.7 0.0 copy-done.3
  120.7 0.1 fusion.8
  120.7 0.7 copy.19
  121.5 0.8 collective-permute-done.5
  122.3 1.8 %collective-permute-start.6 = (f32[1,512,128]{1,2,0:T(8,128)}, f32[1,512,128]{1,2,0:T(8,128)S(1)}, u32[]{:S(2)}, u32[]{:S(2)}) collective-permute-start(f32[1,512,128]{1,2,0:T(8,128)} %collective-permute-done.5), channel_id=1, source_target_pairs={{0,28},{4,0},{8,4},{12,8},{16,12},{20,16},{24,20},{28,24},{1,29},{... | collective-permute-start | bytes 786440 | tf_op jit(solution)/shard_map/ppermute | solution.py:42
  124.1 6.0 %collective-permute-done.3 = f32[1,512,128]{1,2,0:T(8,128)} collective-permute-done((f32[1,512,128]{1,2,0:T(8,128)S(1)}, f32[1,512,128]{1,2,0:T(8,128)}, u32[]{:S(2)}, u32[]{:S(2)}) %collective-permute-start.3) | collective-permute-done | bytes 262176 | tf_op jit(solution)/shard_map/ppermute | solution.py:40
  130.2 1.0 constant_dynamic-update-slice_fusion.15
  131.3 1.0 constant_dynamic-update-slice_fusion.9
  132.2 0.6 collective-permute-done.6
  132.9 1.0 constant_dynamic-update-slice_fusion.7
  134.0 1.0 constant_dynamic-update-slice_fusion.1
  135.0 1.6 constant_dynamic-slice_fusion
  136.6 2.9 %copy.17 = f32[8,512,128]{2,1,0:T(8,128)} copy(f32[8,512,128]{1,2,0:T(8,128)} %constant_dynamic-slice_fusion) | data formatting | bytes 4194304 | tf_op jit(solution)/shard_map/jit(_roll_dynamic)/dynamic_slice | solution.py:44
  139.5 20.4 %gather_fusion.2 = f32[2048,128]{1,0:T(8,128)S(1)} fusion(f32[8,512,128]{2,1,0:T(8,128)} %copy.17, s32[2048]{0:T(1024)S(1)} %bitcast.45), kind=kCustom, calls=%fused_computation.2 | custom fusion | bytes 2113536 | tf_op jit(solution)/shard_map/gather | solution.py:47
  159.9 0.0 copy-start.2
  159.9 0.0 copy-done
  159.9 4.9 %fusion = f32[8,256,128]{2,1,0:T(8,128)S(1)} fusion(f32[8,256,128]{2,1,0:T(8,128)} %param.20, f32[8,256,128]{2,1,0:T(8,128)S(1)} %bitcast.46, f32[8,256,256]{2,1,0:T(8,128)S(1)} %copy-done), kind=kOutput, calls=%fused_computation.5 | convolution fusion | flops 805568512 | bytes 5242880 | tf_op jit(solution)/shard_map/skw,skr->swr/dot_general | solution.py:48
  164.8 0.0 copy-done.2
  164.8 2.0 %convolution_bitcast_fusion = f32[8,256,128]{1,2,0:T(8,128)S(1)} fusion(f32[8,256,128]{2,1,0:T(8,128)S(1)} %fusion, f32[8,256,256]{2,1,0:T(8,128)S(1)} %copy-done.2), kind=kOutput, calls=%fused_computation.3 | convolution fusion | flops 805306368 | bytes 4194304 | tf_op jit(solution)/shard_map/skw,skr->swr/dot_general | solution.py:49
  166.9 1.3 copy.20
  (18 shorter events, 0.3 us)
Async XLA Ops:
  7.2 152.8 %copy-start = (f32[8,256,256]{2,1,0:T(8,128)S(1)}, f32[8,256,256]{2,1,0:T(8,128)}, u32[]{:S(2)}) copy-start(f32[8,256,256]{2,1,0:T(8,128)} %param.19) | copy-start | bytes 6291460
  7.2 88.4 %copy-start.4 = (s32[8]{0:T(128)S(1)}, s32[8]{0:T(128)}, u32[]{:S(2)}) copy-start(s32[8]{0:T(128)} %param.17) | copy-start | bytes 100
  7.2 100.1 %copy-start.1 = (s32[8]{0:T(128)S(1)}, s32[8]{0:T(128)}, u32[]{:S(2)}) copy-start(s32[8]{0:T(128)} %param.16) | copy-start | bytes 100
  7.2 113.5 %copy-start.3 = (s32[8,256]{1,0:T(8,128)S(1)}, s32[8,256]{1,0:T(8,128)}, u32[]{:S(2)}) copy-start(s32[8,256]{1,0:T(8,128)} %param.18) | copy-start | bytes 24580
  7.2 76.8 %all-reduce.2.cloned.1.call-start = ((), (), s32[]{:S(2)}) async-start(), calls=%async_computation | async-start | bytes 524288 | tf_op jit(solution)/shard_map/psum | solution.py:30
  86.1 9.5 %collective-permute-start = (f32[1,512,128]{1,2,0:T(8,128)S(1)}, f32[1,512,128]{1,2,0:T(8,128)S(1)}, u32[]{:S(2)}, u32[]{:S(2)}) collective-permute-start(f32[1,512,128]{1,2,0:T(8,128)S(1)} %bitcast.47), channel_id=1, source_target_pairs={{0,4},{4,8},{8,12},{12,16},{16,20},{20,24},{24,28},{28,0},{1,5},{5... | collective-permute-start | bytes 786440 | tf_op jit(solution)/shard_map/ppermute | solution.py:40
  95.6 9.2 %collective-permute-start.1 = (f32[1,512,128]{1,2,0:T(8,128)S(1)}, f32[1,512,128]{1,2,0:T(8,128)S(1)}, u32[]{:S(2)}, u32[]{:S(2)}) collective-permute-start(f32[1,512,128]{1,2,0:T(8,128)S(1)} %collective-permute-done), channel_id=1, source_target_pairs={{0,4},{4,8},{8,12},{12,16},{16,20},{20,24},{24,28},{28,0},{1,5},{5... | collective-permute-start | bytes 786440 | tf_op jit(solution)/shard_map/ppermute | solution.py:40
  95.6 12.3 %collective-permute-start.4 = (f32[1,512,128]{1,2,0:T(8,128)S(1)}, f32[1,512,128]{1,2,0:T(8,128)S(1)}, u32[]{:S(2)}, u32[]{:S(2)}) collective-permute-start(f32[1,512,128]{1,2,0:T(8,128)S(1)} %bitcast.48), channel_id=1, source_target_pairs={{0,28},{4,0},{8,4},{12,8},{16,12},{20,16},{24,20},{28,24},{1,29},{... | collective-permute-start | bytes 786440 | tf_op jit(solution)/shard_map/ppermute | solution.py:42
  104.8 13.4 %collective-permute-start.2 = (f32[1,512,128]{1,2,0:T(8,128)S(1)}, f32[1,512,128]{1,2,0:T(8,128)S(1)}, u32[]{:S(2)}, u32[]{:S(2)}) collective-permute-start(f32[1,512,128]{1,2,0:T(8,128)S(1)} %collective-permute-done.1), channel_id=1, source_target_pairs={{0,4},{4,8},{8,12},{12,16},{16,20},{20,24},{24,28},{28,0},{1,5},{5... | collective-permute-start | bytes 786440 | tf_op jit(solution)/shard_map/ppermute | solution.py:40
  108.0 14.3 %collective-permute-start.5 = (f32[1,512,128]{1,2,0:T(8,128)S(1)}, f32[1,512,128]{1,2,0:T(8,128)}, u32[]{:S(2)}, u32[]{:S(2)}) collective-permute-start(f32[1,512,128]{1,2,0:T(8,128)S(1)} %collective-permute-done.4), channel_id=1, source_target_pairs={{0,28},{4,0},{8,4},{12,8},{16,12},{20,16},{24,20},{28,24},{1,29},{... | collective-permute-start | bytes 786440 | tf_op jit(solution)/shard_map/ppermute | solution.py:42
  118.2 12.0 %collective-permute-start.3 = (f32[1,512,128]{1,2,0:T(8,128)S(1)}, f32[1,512,128]{1,2,0:T(8,128)}, u32[]{:S(2)}, u32[]{:S(2)}) collective-permute-start(f32[1,512,128]{1,2,0:T(8,128)S(1)} %collective-permute-done.2), channel_id=1, source_target_pairs={{0,4},{4,8},{8,12},{12,16},{16,20},{20,24},{24,28},{28,0},{1,5},{5... | collective-permute-start | bytes 786440 | tf_op jit(solution)/shard_map/ppermute | solution.py:40
  122.3 10.6 %collective-permute-start.6 = (f32[1,512,128]{1,2,0:T(8,128)}, f32[1,512,128]{1,2,0:T(8,128)S(1)}, u32[]{:S(2)}, u32[]{:S(2)}) collective-permute-start(f32[1,512,128]{1,2,0:T(8,128)} %collective-permute-done.5), channel_id=1, source_target_pairs={{0,28},{4,0},{8,4},{12,8},{16,12},{20,16},{24,20},{28,24},{1,29},{... | collective-permute-start | bytes 786440 | tf_op jit(solution)/shard_map/ppermute | solution.py:42
  159.9 4.9 %copy-start.2 = (f32[8,256,256]{2,1,0:T(8,128)S(1)}, f32[8,256,256]{2,1,0:T(8,128)}, u32[]{:S(2)}) copy-start(f32[8,256,256]{2,1,0:T(8,128)} %param.21) | copy-start | bytes 6291460
Sparse Core Ops, SparseCore 0:
  55.9 28.0 all-reduce.1
